TPU v7x, 32 devices: a whole 2x2x4 slice. The times are simulated.
32 devices in a mesh: shard: 8 (over z, x), tensor: 4 (over y, core).
Axes of the slice: x: 2, y: 2, z: 4, core: 2. Of those that a mesh axis runs over, the one named last changes fastest.
Arguments:
- wide_weight: bfloat16 [4, 4096, 4096], P(None, 'shard', 'tensor'), may hold values from -6 to 6
- wide_grad: bfloat16 [4, 4096, 4096], P(None, 'shard', 'tensor'), may hold values from -6 to 6
- wide_first: float32 [4, 4096, 256], P(None, ('shard', 'tensor')), may hold values from -4 to 4
- wide_second: float32 [4, 4096, 256], P(None, ('shard', 'tensor')), may hold values from 0.001 to 0.1
- wide_basis: bfloat16 [4, 4096, 256], P(None, 'tensor'), may hold values from -0.09375 to 0.09375
- narrow_weight: bfloat16 [4, 1024, 4096], P(None, 'shard', 'tensor'), may hold values from -6 to 6
- narrow_grad: bfloat16 [4, 1024, 4096], P(None, 'shard', 'tensor'), may hold values from -6 to 6
- narrow_first: float32 [4, 1024, 256], P(None, ('shard', 'tensor')), may hold values from -4 to 4
- narrow_second: float32 [4, 1024, 256], P(None, ('shard', 'tensor')), may hold values from 0.001 to 0.1
- narrow_basis: bfloat16 [4, 4096, 256], P(None, 'tensor'), may hold values from -0.09375 to 0.09375
- vocab_weight: bfloat16 [2, 32000, 4096], P(None, 'shard', 'tensor'), may hold values from -6 to 6
- vocab_grad: bfloat16 [2, 32000, 4096], P(None, 'shard', 'tensor'), may hold values from -6 to 6
- vocab_first: float32 [2, 32000, 256], P(None, ('shard', 'tensor')), may hold values from -4 to 4
- vocab_second: float32 [2, 32000, 256], P(None, ('shard', 'tensor')), may hold values from 0.001 to 0.1
- vocab_basis: bfloat16 [2, 4096, 256], P(None, 'tensor'), may hold values from -0.09375 to 0.09375
Outputs:
- wide_weight_new: bfloat16 [4, 4096, 4096], P(None, 'shard', 'tensor')
- wide_first_new: float32 [4, 4096, 256], P(None, ('shard', 'tensor'))
- wide_second_new: float32 [4, 4096, 256], P(None, ('shard', 'tensor'))
- narrow_weight_new: bfloat16 [4, 1024, 4096], P(None, 'shard', 'tensor')
- narrow_first_new: float32 [4, 1024, 256], P(None, ('shard', 'tensor'))
- narrow_second_new: float32 [4, 1024, 256], P(None, ('shard', 'tensor'))
- vocab_weight_new: bfloat16 [2, 32000, 4096], P(None, 'shard', 'tensor')
- vocab_first_new: float32 [2, 32000, 256], P(None, ('shard', 'tensor'))
- vocab_second_new: float32 [2, 32000, 256], P(None, ('shard', 'tensor'))
All inputs are finite; a program needn't handle non-finite values.
Results may differ from a plain program's by a relative error of at most 0.01.
Values may be sent and summed in bfloat16 or wider, within the bound.
No kernel may reach another device: no remote copies, remote signals or barrier semaphores. Data moves between devices by JAX's collectives and lax.ppermute only.
A program may use at most 192 MiB of HBM per device.

v0:
```python
import jax
import jax.numpy as jnp
from jax import lax
from jax.sharding import PartitionSpec as P

NS_ITERS = 3
HIGHEST = lax.Precision.HIGHEST


def local_gram(polish):
    return jnp.einsum("sdk,sdl->skl", polish, polish, precision=HIGHEST)


def polish_small(back, gram):
    trace = jnp.einsum("skk->s", gram)
    scale = 1.0 / jnp.sqrt(trace + 1e-06)
    small = gram * (scale * scale)[:, None, None]
    rank = gram.shape[1]
    eye = jnp.eye(rank, dtype=jnp.float32)[None, :, :]
    factor = jnp.broadcast_to(eye, gram.shape)
    for step in range(NS_ITERS):
        square = jnp.einsum("skl,slm->skm", small, small, precision=HIGHEST)
        turn = 3.4445 * eye - 4.775 * small + 2.0315 * square
        factor = jnp.einsum("skl,slm->skm", factor, turn, precision=HIGHEST)
        if step + 1 < NS_ITERS:
            small = jnp.einsum(
                "skl,slm->skm",
                turn,
                jnp.einsum("skl,slm->skm", small, turn, precision=HIGHEST),
                precision=HIGHEST,
            )
    return jnp.einsum("sdk,skl->sdl", back * scale[:, None, None], factor, precision=HIGHEST)


def adam_moments(first, second, projected):
    first_new = 0.9 * first + 0.1 * projected
    second_new = 0.999 * second + 0.001 * projected * projected
    direction = first_new / (1.0 - 0.9**10) / (jnp.sqrt(second_new / (1.0 - 0.999**10)) + 1e-08)
    return (first_new, second_new, direction.astype(jnp.bfloat16))


def per_device(
    wide_weight,
    wide_grad,
    wide_first,
    wide_second,
    wide_basis,
    narrow_weight,
    narrow_grad,
    narrow_first,
    narrow_second,
    narrow_basis,
    vocab_weight,
    vocab_grad,
    vocab_first,
    vocab_second,
    vocab_basis,
):
    weights = (wide_weight, narrow_weight, vocab_weight)
    grads = (wide_grad, narrow_grad, vocab_grad)
    firsts = (wide_first, narrow_first, vocab_first)
    seconds = (wide_second, narrow_second, vocab_second)
    olds = (wide_basis, narrow_basis, vocab_basis)
    sketch_terms = [
        jnp.einsum("smc,scr->smr", grad, old, preferred_element_type=jnp.float32)
        for grad, old in zip(grads, olds)
    ]
    sketch_sum = (
        lax.psum(sketch_terms[0].astype(jnp.bfloat16), "tensor").astype(jnp.float32),
        lax.psum(sketch_terms[1].astype(jnp.bfloat16), "tensor").astype(jnp.float32),
        lax.psum(sketch_terms[2].astype(jnp.bfloat16), "tensor").astype(jnp.float32),
    )
    sketches = [item.astype(jnp.bfloat16) for item in sketch_sum]
    back_terms = [
        jnp.einsum("smc,smr->scr", grad, sketch, preferred_element_type=jnp.float32)
        for grad, sketch in zip(grads, sketches)
    ]
    backs = (
        lax.psum_scatter(back_terms[0], "shard", scatter_dimension=1, tiled=True),
        lax.psum_scatter(back_terms[1], "shard", scatter_dimension=1, tiled=True),
        lax.psum_scatter(back_terms[2], "shard", scatter_dimension=1, tiled=True),
    )
    first_grams = lax.psum(tuple((local_gram(back) for back in backs)), ("shard", "tensor"))
    rounded = [
        polish_small(back, gram).astype(jnp.bfloat16) for back, gram in zip(backs, first_grams)
    ]
    bases = (
        lax.all_gather(rounded[0], "shard", axis=1, tiled=True),
        lax.all_gather(rounded[1], "shard", axis=1, tiled=True),
        lax.all_gather(rounded[2], "shard", axis=1, tiled=True),
    )
    proj_terms = [
        jnp.einsum("smc,scr->smr", grad, basis, preferred_element_type=jnp.float32)
        for grad, basis in zip(grads, bases)
    ]
    projected = (
        lax.psum_scatter(proj_terms[0], "tensor", scatter_dimension=1, tiled=True),
        lax.psum_scatter(proj_terms[1], "tensor", scatter_dimension=1, tiled=True),
        lax.psum_scatter(proj_terms[2], "tensor", scatter_dimension=1, tiled=True),
    )
    results = [
        adam_moments(first, second, proj) for first, second, proj in zip(firsts, seconds, projected)
    ]
    directions = (
        lax.all_gather(results[0][2], "tensor", axis=1, tiled=True),
        lax.all_gather(results[1][2], "tensor", axis=1, tiled=True),
        lax.all_gather(results[2][2], "tensor", axis=1, tiled=True),
    )
    outputs = []
    for weight, direction, basis, result in zip(weights, directions, bases, results):
        update = jnp.einsum("smr,scr->smc", direction, basis, preferred_element_type=jnp.float32)
        weight_new = (0.99 * weight.astype(jnp.float32) - 2.0 * update).astype(jnp.bfloat16)
        outputs.append((weight_new, result[0], result[1]))
    return (
        outputs[0][0],
        outputs[0][1],
        outputs[0][2],
        outputs[1][0],
        outputs[1][1],
        outputs[1][2],
        outputs[2][0],
        outputs[2][1],
        outputs[2][2],
    )


def solution(mesh):
    in_specs = (
        P(None, "shard", "tensor"),
        P(None, "shard", "tensor"),
        P(None, ("shard", "tensor"), None),
        P(None, ("shard", "tensor"), None),
        P(None, "tensor", None),
        P(None, "shard", "tensor"),
        P(None, "shard", "tensor"),
        P(None, ("shard", "tensor"), None),
        P(None, ("shard", "tensor"), None),
        P(None, "tensor", None),
        P(None, "shard", "tensor"),
        P(None, "shard", "tensor"),
        P(None, ("shard", "tensor"), None),
        P(None, ("shard", "tensor"), None),
        P(None, "tensor", None),
    )
    out_specs = (
        P(None, "shard", "tensor"),
        P(None, ("shard", "tensor"), None),
        P(None, ("shard", "tensor"), None),
        P(None, "shard", "tensor"),
        P(None, ("shard", "tensor"), None),
        P(None, ("shard", "tensor"), None),
        P(None, "shard", "tensor"),
        P(None, ("shard", "tensor"), None),
        P(None, ("shard", "tensor"), None),
    )
    return jax.shard_map(
        per_device, mesh=mesh, in_specs=in_specs, out_specs=out_specs, check_vma=False
    )
```

profile of v0, /device:TPU:0, one launch (start us, length us, event | category | flops | bytes accessed | tf_op | source)
XLA Modules:
  0.0 922.7 jit_solution(10910709305503595160)
XLA Ops:
  7.2 12.4 %convolution_convert_fusion = bf16[2,4000,256]{2,1,0:T(8,128)(2,1)} fusion(bf16[2,4000,1024]{2,1,0:T(8,128)(2,1)} %param.26, bf16[2,1024,256]{2,1,0:T(8,128)(2,1)} %param.29), kind=kOutput, calls=%fused_computation.3 | convolution fusion | flops 4196352000 | bytes 21528576 | tf_op jit(solution)/shard_map/smc,scr->smr/dot_general | solution.py:65
  19.7 4.6 convolution_convert_fusion.1
  26.0 108.4 %all-reduce.11.cloned.1.call-done = (bf16[4,512,256]{1,2,0:T(8,128)(2,1)}, bf16[4,128,256]{1,2,0:T(8,128)(2,1)}, bf16[2,4000,256]{2,1,0:T(8,128)(2,1)}) async-done(((bf16[4,512,256]{1,2,0:T(8,128)(2,1)}, bf16[4,128,256]{1,2,0:T(8,128)(2,1)}, bf16[2,4000,256]{2,1,0:T(8,128)(2,1)}), (bf16[4,512,256]{1,2,0:T(8,128)(2,1)}, bf16[4,128,256]{1,2,0:T(8,128)(2,1)}, ...) | async-done | bytes 5406736 | tf_op jit(solution)/shard_map/psum | solution.py:69
  134.3 12.8 %convolution_bitcast_fusion.3 = f32[2,1024,256]{1,2,0:T(8,128)} fusion(bf16[2,4000,256]{2,1,0:T(8,128)(2,1)} %get-tuple-element.34, bf16[2,4000,1024]{2,1,0:T(8,128)(2,1)} %param.26), kind=kOutput, calls=%fused_computation.11 | convolution fusion | flops 4194304000 | bytes 22577152 | tf_op jit(solution)/shard_map/smc,smr->scr/dot_general | solution.py:75
  148.4 5.5 convolution_bitcast_fusion.2
  154.8 2.7 convolution_bitcast_fusion.1
  157.6 58.0 %reduce-scatter.12.cloned.1.call-done = f32[2,128,256]{1,2,0:T(8,128)} async-done(((f32[2,1024,256]{1,2,0:T(8,128)}), f32[2,128,256]{1,2,0:T(8,128)}) %reduce-scatter.12.cloned.1.call-update) | async-done | bytes 262160 | tf_op jit(solution)/shard_map/reduce_scatter | solution.py:81
  215.6 2.4 fusion.63
  218.0 89.7 %reduce-scatter.6.cloned.1.call-done = f32[4,128,256]{1,2,0:T(8,128)} async-done(((f32[4,1024,256]{1,2,0:T(8,128)}), f32[4,128,256]{1,2,0:T(8,128)}) %reduce-scatter.6.cloned.1.call-update) | async-done | bytes 524304 | tf_op jit(solution)/shard_map/reduce_scatter | solution.py:79
  307.7 3.2 fusion.51
  310.8 89.0 %reduce-scatter.10.cloned.1.call-done = f32[4,128,256]{1,2,0:T(8,128)} async-done(((f32[4,1024,256]{1,2,0:T(8,128)}), f32[4,128,256]{1,2,0:T(8,128)}) %reduce-scatter.10.cloned.1.call-update) | async-done | bytes 524304 | tf_op jit(solution)/shard_map/reduce_scatter | solution.py:80
  399.8 3.2 fusion.57
  403.2 141.4 %all-reduce.9.cloned.1.call-done = (f32[4,256,256]{2,1,0:T(8,128)}, f32[4,256,256]{2,1,0:T(8,128)}, f32[2,256,256]{2,1,0:T(8,128)}) async-done(((f32[4,256,256]{2,1,0:T(8,128)}, f32[4,256,256]{2,1,0:T(8,128)}, f32[2,256,256]{2,1,0:T(8,128)}), (f32[4,256,256]{2,1,0:T(8,128)}, f32[4,256,256]{2,1,0:T(8,128)}, f32[2,256,256]{2,1,0:T(8,128)})) %all-reduce.9.cloned.1.call-update) | async-done | bytes 2621456 | tf_op jit(solution)/shard_map/psum | solution.py:83
  545.9 2.2 fusion.9
  576.6 2.0 fusion.22
  586.4 25.7 %all-gather.6.cloned.1.call-done = bf16[4,1024,256]{2,1,0:T(8,128)(2,1)} async-done(((bf16[4,128,256]{2,1,0:T(8,128)(2,1)}), bf16[4,1024,256]{2,1,0:T(8,128)(2,1)}) %all-gather.6.cloned.1.call-update) | async-done | bytes 2097168 | tf_op jit(solution)/shard_map/all_gather | solution.py:88
  612.2 5.5 convolution_bitcast_fusion.4
  618.2 35.5 %all-gather.12.cloned.1.call-done = bf16[2,1024,256]{2,1,0:T(8,128)(2,1)} async-done(((bf16[2,128,256]{2,1,0:T(8,128)(2,1)}), bf16[2,1024,256]{2,1,0:T(8,128)(2,1)}) %all-gather.12.cloned.1.call-update) | async-done | bytes 1048592 | tf_op jit(solution)/shard_map/all_gather | solution.py:90
  653.6 13.6 %convolution_bitcast_fusion = f32[2,4000,256]{2,1,0:T(8,128)} fusion(bf16[2,4000,1024]{2,1,0:T(8,128)(2,1)} %param.26, bf16[2,1024,256]{2,1,0:T(8,128)(2,1)} %all-gather.12.cloned.1.call-done), kind=kOutput, calls=%fused_computation.2 | convolution fusion | flops 4194304000 | bytes 25624576 | tf_op jit(solution)/shard_map/smc,scr->smr/dot_general | solution.py:93
  669.5 34.9 %all-gather.10.cloned.1.call-done = bf16[4,1024,256]{2,1,0:T(8,128)(2,1)} async-done(((bf16[4,128,256]{2,1,0:T(8,128)(2,1)}), bf16[4,1024,256]{2,1,0:T(8,128)(2,1)}) %all-gather.10.cloned.1.call-update) | async-done | bytes 2097168 | tf_op jit(solution)/shard_map/all_gather | solution.py:89
  704.4 2.4 convolution_bitcast_fusion.5
  708.0 29.6 %reduce-scatter.8.cloned.1.call-done = f32[4,128,256]{1,2,0:T(8,128)} async-done(((f32[4,512,256]{1,2,0:T(8,128)}), f32[4,128,256]{1,2,0:T(8,128)}) %reduce-scatter.8.cloned.1.call-update) | async-done | bytes 524304 | tf_op jit(solution)/shard_map/reduce_scatter | solution.py:97
  737.5 2.3 divide_convert_fusion.1
  739.9 71.4 %reduce-scatter.14.cloned.1.call-done = f32[2,1000,256]{2,1,0:T(8,128)} async-done(((f32[2,4000,256]{2,1,0:T(8,128)}), f32[2,1000,256]{2,1,0:T(8,128)}) %reduce-scatter.14.cloned.1.call-update) | async-done | bytes 2048016 | tf_op jit(solution)/shard_map/reduce_scatter | solution.py:99
  811.3 6.0 divide_convert_fusion
  818.6 29.0 %all-reduce.7.cloned.1.call-done = f32[4,128,256]{2,0,1:T(4,128)} async-done(((f32[4,128,256]{2,0,1:T(4,128)}), f32[4,128,256]{2,0,1:T(4,128)}) %all-reduce.7.cloned.1.call-update) | async-done | bytes 524304
  850.1 5.9 all_gather.21
  856.1 3.0 subtract_convert_fusion.2
  861.1 5.4 all-gather.8.cloned.1.call-done
  866.5 6.4 subtract_convert_fusion.1
  872.9 29.8 %all-gather.14.cloned.1.call-done = bf16[2,4000,256]{2,1,0:T(8,128)(2,1)} async-done(((bf16[2,1000,256]{2,1,0:T(8,128)(2,1)}), bf16[2,4000,256]{2,1,0:T(8,128)(2,1)}) %all-gather.14.cloned.1.call-update) | async-done | bytes 4096016 | tf_op jit(solution)/shard_map/all_gather | solution.py:107
  902.7 13.3 %subtract_convert_fusion = bf16[2,4000,1024]{2,1,0:T(8,128)(2,1)} fusion(bf16[2,4000,1024]{2,1,0:T(8,128)(2,1)} %param.25, bf16[2,4000,256]{2,1,0:T(8,128)(2,1)} %all-gather.14.cloned.1.call-done, bf16[2,1024,256]{2,1,0:T(8,128)(2,1)S(1)} %copy-done.20), kind=kOutput, calls=%fused_computation | convolution fusion | flops 4235264000 | bytes 37912576 | tf_op jit(solution)/shard_map/smr,scr->smc/dot_general | solution.py:111
  (118 shorter events, 50.4 us)
Async XLA Ops:
  7.2 12.5 %copy-start = (bf16[4,1024,256]{2,1,0:T(8,128)(2,1)S(1)}, bf16[4,1024,256]{2,1,0:T(8,128)(2,1)}, u32[]{:S(2)}) copy-start(bf16[4,1024,256]{2,1,0:T(8,128)(2,1)} %param.19) | copy-start | bytes 6291460
  7.2 127.1 %all-reduce.11.cloned.1.call-start = ((), (), s32[]{:S(2)}) async-start(), calls=%async_computation.17 | async-start | bytes 10813440 | tf_op jit(solution)/shard_map/psum | solution.py:69
  19.7 4.6 copy-start.2
  19.7 4.6 copy-start.12
  25.9 189.7 %reduce-scatter.12.cloned.1.call-start = ((), (), s32[]{:S(2)}) async-start(), calls=%async_computation.11 | async-start | bytes 2359296 | tf_op jit(solution)/shard_map/reduce_scatter | solution.py:81
  147.1 1.2 copy-start.14
  147.2 160.5 %reduce-scatter.6.cloned.1.call-start = ((), (), s32[]{:S(2)}) async-start(), calls=%async_computation.5 | async-start | bytes 4718592 | tf_op jit(solution)/shard_map/reduce_scatter | solution.py:79
  153.9 246.0 %reduce-scatter.10.cloned.1.call-start = ((), (), s32[]{:S(2)}) async-start(), calls=%async_computation.9 | async-start | bytes 4718592 | tf_op jit(solution)/shard_map/reduce_scatter | solution.py:80
  157.6 387.0 %all-reduce.9.cloned.1.call-start = ((), (), s32[]{:S(2)}) async-start(), calls=%async_computation.16 | async-start | bytes 5242880 | tf_op jit(solution)/shard_map/psum | solution.py:83
  403.0 209.1 %all-gather.6.cloned.1.call-start = ((), (), s32[]{:S(2)}) async-start(), calls=%async_computation.6 | async-start | bytes 2359296 | tf_op jit(solution)/shard_map/all_gather | solution.py:88
  403.1 160.8 %copy-start.10 = (f32[256,256]{1,0:T(8,128)}, f32[256,256]{1,0:T(8,128)S(1)}, u32[]{:S(2)}) copy-start(f32[256,256]{1,0:T(8,128)S(1)} %fusion.38) | copy-start | bytes 786436
  544.5 3.6 copy-start.4
  544.5 5.2 copy-start.5
  560.8 1.2 copy-start.9
  562.0 2.6 copy-start.7
  563.9 89.8 %all-gather.12.cloned.1.call-start = ((), (), s32[]{:S(2)}) async-start(), calls=%async_computation.12 | async-start | bytes 1179648 | tf_op jit(solution)/shard_map/all_gather | solution.py:90
  568.6 1.4 copy-start.11
  576.3 128.1 %all-gather.10.cloned.1.call-start = ((), (), s32[]{:S(2)}) async-start(), calls=%async_computation.10 | async-start | bytes 2359296 | tf_op jit(solution)/shard_map/all_gather | solution.py:89
  586.4 151.1 %reduce-scatter.8.cloned.1.call-start = ((), (), s32[]{:S(2)}) async-start(), calls=%async_computation.7 | async-start | bytes 2621440 | tf_op jit(solution)/shard_map/reduce_scatter | solution.py:97
  617.7 193.5 %reduce-scatter.14.cloned.1.call-start = ((), (), s32[]{:S(2)}) async-start(), calls=%async_computation.13 | async-start | bytes 10240000 | tf_op jit(solution)/shard_map/reduce_scatter | solution.py:99
  667.3 1.2 copy-start.16
  667.3 37.1 %copy-start.3 = (bf16[4,128,1024]{2,1,0:T(8,128)(2,1)S(1)}, bf16[4,128,1024]{2,1,0:T(8,128)(2,1)}, u32[]{:S(2)}) copy-start(bf16[4,128,1024]{2,1,0:T(8,128)(2,1)} %param.21) | copy-start | bytes 3145732
  667.3 180.2 %all-reduce.7.cloned.1.call-start = ((), (), s32[]{:S(2)}) async-start(), calls=%async_computation.15 | async-start | bytes 1048576
  707.9 158.6 %all-gather.8.cloned.1.call-start = ((), (), s32[]{:S(2)}) async-start(), calls=%async_computation.8 | async-start | bytes 1310720 | tf_op jit(solution)/shard_map/all_gather | solution.py:105
  739.8 77.5 %copy-start.21 = (u32[32]{0:T(128)S(1)}, u32[32]{0:T(128)}, u32[]{:S(2)}) copy-start(u32[32]{0:T(128)} %constant.11) | copy-start | bytes 388
  739.8 107.7 %copy-start.18 = (f32[4,32,256]{2,1,0:T(8,128)S(1)}, f32[4,32,256]{2,1,0:T(8,128)}, u32[]{:S(2)}) copy-start(f32[4,32,256]{2,1,0:T(8,128)} %param.22) | copy-start | bytes 393220
  739.8 107.7 %copy-start.19 = (f32[4,32,256]{2,1,0:T(8,128)S(1)}, f32[4,32,256]{2,1,0:T(8,128)}, u32[]{:S(2)}) copy-start(f32[4,32,256]{2,1,0:T(8,128)} %param.23) | copy-start | bytes 393220
  739.8 162.8 %all-gather.14.cloned.1.call-start = ((), (), s32[]{:S(2)}) async-start(), calls=%async_computation.14 | async-start | bytes 5120000 | tf_op jit(solution)/shard_map/all_gather | solution.py:107
  817.3 38.8 %copy-start.6 = (bf16[4,1024,256]{2,1,0:T(8,128)(2,1)S(1)}, bf16[4,1024,256]{2,1,0:T(8,128)(2,1)}, u32[]{:S(2)}) copy-start(bf16[4,1024,256]{2,1,0:T(8,128)(2,1)} %all-gather.10.cloned.1.call-done) | copy-start | bytes 6291460
  859.1 7.4 copy-start.13
  861.1 41.6 %copy-start.20 = (bf16[2,1024,256]{2,1,0:T(8,128)(2,1)S(1)}, bf16[2,1024,256]{2,1,0:T(8,128)(2,1)}, u32[]{:S(2)}) copy-start(bf16[2,1024,256]{2,1,0:T(8,128)(2,1)} %all-gather.12.cloned.1.call-done) | copy-start | bytes 3145732
  902.6 13.3 %copy-start.1 = (bf16[4,1024,256]{2,1,0:T(8,128)(2,1)S(1)}, bf16[4,1024,256]{2,1,0:T(8,128)(2,1)}, u32[]{:S(2)}) copy-start(bf16[4,1024,256]{2,1,0:T(8,128)(2,1)} %param.19) | copy-start | bytes 6291460
  (3 other events, 3.2 us)
Sparse Core Ops, SparseCore 0:
  26.0 108.2 all-reduce.10
  147.3 68.2 reduce-scatter.11
  220.2 87.4 reduce-scatter.5
  311.7 88.0 reduce-scatter.9
  407.6 136.8 all-reduce.8
  564.0 48.1 all-gather.5
  614.9 38.6 all-gather.11
  656.4 48.0 all-gather.9
  707.5 29.9 reduce-scatter.7
  740.8 70.4 reduce-scatter.13
  814.3 33.1 all-reduce.6
  849.6 16.8 all-gather.7
  868.7 33.9 all-gather.13
where the time goes:
time: 931 us; the launch traced here: 923 us
  waiting for transfers between devices  748 us (80%)
  matrix products  131 us (14%)
  between operations  15.2 us (2%)
  other arithmetic  12.5 us (1%)
    psum x1, waiting for transfers between devices, per_device(): lax.psum(tuple((local_gram(back) for back in backs)), ('shard', 'tensor'))  141 us
    psum x1, waiting for transfers between devices, per_device(): lax.psum(sketch_terms[0].astype(jnp.bfloat16), 'tensor').astype(jnp.float32)  108 us
    reduce_scatter x1, waiting for transfers between devices, per_device(): lax.psum_scatter(back_terms[0], 'shard', scatter_dimension=1, tiled=True)  89.7 us
    reduce_scatter x1, waiting for transfers between devices, per_device(): lax.psum_scatter(back_terms[1], 'shard', scatter_dimension=1, tiled=True)  89 us
    reduce_scatter x1, waiting for transfers between devices, per_device(): lax.psum_scatter(proj_terms[2], 'tensor', scatter_dimension=1, tiled=True)  71.4 us
    reduce_scatter x1, waiting for transfers between devices, per_device(): lax.psum_scatter(back_terms[2], 'shard', scatter_dimension=1, tiled=True)  58 us
    all_gather x1, waiting for transfers between devices, per_device(): lax.all_gather(rounded[2], 'shard', axis=1, tiled=True)  35.5 us
    all_gather x1, waiting for transfers between devices, per_device(): lax.all_gather(rounded[1], 'shard', axis=1, tiled=True)  34.9 us
  transfers between devices with their start and end apart: 13, of which 13 were waited for; matrix products, arithmetic and copies ran while one was open for 9% of the time, Pallas kernels for 0%

commit v1 on v0

--- a/solution.py
+++ b/solution.py
@@ -2,6 +2,7 @@
 import jax.numpy as jnp
 from jax import lax
 from jax.sharding import PartitionSpec as P
+from jax.lax import psum
 
 NS_ITERS = 3
 HIGHEST = lax.Precision.HIGHEST
@@ -80,7 +81,7 @@
         lax.psum_scatter(back_terms[1], "shard", scatter_dimension=1, tiled=True),
         lax.psum_scatter(back_terms[2], "shard", scatter_dimension=1, tiled=True),
     )
-    first_grams = lax.psum(tuple((local_gram(back) for back in backs)), ("shard", "tensor"))
+    first_grams = psum(psum(tuple((local_gram(back) for back in backs)), "tensor"), "shard")
     rounded = [
         polish_small(back, gram).astype(jnp.bfloat16) for back, gram in zip(backs, first_grams)
     ]

time: 931 us -> 972 us (1.044)
  waiting for transfers between devices: 748 us -> 788 us
    psum x1 -> x2, waiting for transfers between devices: 141 us -> 181 us  [the longest x1 121 us: per_device(): psum(psum(tuple((local_gram(back) for back in backs)), 'tensor'), 'shard')]
    unnamed x14 -> x15, waiting for transfers between devices: 29.2 us -> 29 us
  transfers between devices with their start and end apart: 13 -> 14, of which waited for: 13 -> 14; matrix products, arithmetic and copies ran while one was open for 9% -> 9% of each run, Pallas kernels for 0% -> 0%
where the time goes in v1:
time: 972 us; the launch traced here: 963 us
  waiting for transfers between devices  788 us (81%)
  matrix products  131 us (13%)
  between operations  15.2 us (2%)
  other arithmetic  12.5 us (1%)
    psum x1, waiting for transfers between devices, per_device(): psum(psum(tuple((local_gram(back) for back in backs)), 'tensor'), 'shard')  121 us
    psum x1, waiting for transfers between devices, per_device(): lax.psum(sketch_terms[0].astype(jnp.bfloat16), 'tensor').astype(jnp.float32)  108 us
    reduce_scatter x1, waiting for transfers between devices, per_device(): lax.psum_scatter(back_terms[0], 'shard', scatter_dimension=1, tiled=True)  89.7 us
    reduce_scatter x1, waiting for transfers between devices, per_device(): lax.psum_scatter(back_terms[1], 'shard', scatter_dimension=1, tiled=True)  89 us
    reduce_scatter x1, waiting for transfers between devices, per_device(): lax.psum_scatter(proj_terms[2], 'tensor', scatter_dimension=1, tiled=True)  71.4 us
    psum x1, waiting for transfers between devices, per_device(): psum(tuple((local_gram(back) for back in backs)), 'tensor')  60.5 us
    reduce_scatter x1, waiting for transfers between devices, per_device(): lax.psum_scatter(back_terms[2], 'shard', scatter_dimension=1, tiled=True)  58 us
    all_gather x1, waiting for transfers between devices, per_device(): lax.all_gather(rounded[2], 'shard', axis=1, tiled=True)  35.7 us
  transfers between devices with their start and end apart: 14, of which 14 were waited for; matrix products, arithmetic and copies ran while one was open for 9% of the time, Pallas kernels for 0%

profile of v1, /device:TPU:0, one launch (start us, length us, event | category | flops | bytes accessed | tf_op | source)
XLA Modules:
  0.0 963.1 jit_solution(6798096311011465155)
XLA Ops:
  7.2 12.4 %convolution_convert_fusion = bf16[2,4000,256]{2,1,0:T(8,128)(2,1)} fusion(bf16[2,4000,1024]{2,1,0:T(8,128)(2,1)} %param.26, bf16[2,1024,256]{2,1,0:T(8,128)(2,1)} %param.29), kind=kOutput, calls=%fused_computation.3 | convolution fusion | flops 4196352000 | bytes 21528576 | tf_op jit(solution)/shard_map/smc,scr->smr/dot_general | solution.py:66
  19.7 4.6 convolution_convert_fusion.1
  26.0 108.4 %all-reduce.15.cloned.1.call-done = (bf16[4,512,256]{1,2,0:T(8,128)(2,1)}, bf16[4,128,256]{1,2,0:T(8,128)(2,1)}, bf16[2,4000,256]{2,1,0:T(8,128)(2,1)}) async-done(((bf16[4,512,256]{1,2,0:T(8,128)(2,1)}, bf16[4,128,256]{1,2,0:T(8,128)(2,1)}, bf16[2,4000,256]{2,1,0:T(8,128)(2,1)}), (bf16[4,512,256]{1,2,0:T(8,128)(2,1)}, bf16[4,128,256]{1,2,0:T(8,128)(2,1)}, ...) | async-done | bytes 5406736 | tf_op jit(solution)/shard_map/psum | solution.py:70
  134.3 12.8 %convolution_bitcast_fusion.3 = f32[2,1024,256]{1,2,0:T(8,128)} fusion(bf16[2,4000,256]{2,1,0:T(8,128)(2,1)} %get-tuple-element.37, bf16[2,4000,1024]{2,1,0:T(8,128)(2,1)} %param.26), kind=kOutput, calls=%fused_computation.11 | convolution fusion | flops 4194304000 | bytes 22577152 | tf_op jit(solution)/shard_map/smc,smr->scr/dot_general | solution.py:76
  148.4 5.5 convolution_bitcast_fusion.2
  154.8 2.7 convolution_bitcast_fusion.1
  157.6 58.0 %reduce-scatter.12.cloned.1.call-done = f32[2,128,256]{1,2,0:T(8,128)} async-done(((f32[2,1024,256]{1,2,0:T(8,128)}), f32[2,128,256]{1,2,0:T(8,128)}) %reduce-scatter.12.cloned.1.call-update) | async-done | bytes 262160 | tf_op jit(solution)/shard_map/reduce_scatter | solution.py:82
  215.6 2.4 fusion.63
  218.0 89.7 %reduce-scatter.6.cloned.1.call-done = f32[4,128,256]{1,2,0:T(8,128)} async-done(((f32[4,1024,256]{1,2,0:T(8,128)}), f32[4,128,256]{1,2,0:T(8,128)}) %reduce-scatter.6.cloned.1.call-update) | async-done | bytes 524304 | tf_op jit(solution)/shard_map/reduce_scatter | solution.py:80
  307.7 3.2 fusion.51
  310.9 89.0 %reduce-scatter.10.cloned.1.call-done = f32[4,128,256]{1,2,0:T(8,128)} async-done(((f32[4,1024,256]{1,2,0:T(8,128)}), f32[4,128,256]{1,2,0:T(8,128)}) %reduce-scatter.10.cloned.1.call-update) | async-done | bytes 524304 | tf_op jit(solution)/shard_map/reduce_scatter | solution.py:81
  399.8 3.2 fusion.57
  403.1 60.5 %all-reduce.13.cloned.1.call-done = (f32[4,256,256]{2,1,0:T(8,128)}, f32[4,256,256]{2,1,0:T(8,128)}, f32[2,256,256]{2,1,0:T(8,128)}) async-done(((f32[4,256,256]{2,1,0:T(8,128)}, f32[4,256,256]{2,1,0:T(8,128)}, f32[2,256,256]{2,1,0:T(8,128)}), (f32[4,256,256]{2,1,0:T(8,128)}, f32[4,256,256]{2,1,0:T(8,128)}, f32[2,256,256]{2,1,0:T(8,128)})) %all-reduce.13.cloned.1.call-update) | async-done | bytes 2621456 | tf_op jit(solution)/shard_map/psum | solution.py:84
  463.8 120.8 %all-reduce.11.cloned.1.call-done = (f32[4,256,256]{2,1,0:T(8,128)}, f32[4,256,256]{2,1,0:T(8,128)}, f32[2,256,256]{2,1,0:T(8,128)}) async-done(((f32[4,256,256]{2,1,0:T(8,128)}, f32[4,256,256]{2,1,0:T(8,128)}, f32[2,256,256]{2,1,0:T(8,128)}), (f32[4,256,256]{2,1,0:T(8,128)}, f32[4,256,256]{2,1,0:T(8,128)}, f32[2,256,256]{2,1,0:T(8,128)})) %all-reduce.11.cloned.1.call-update) | async-done | bytes 2621456 | tf_op jit(solution)/shard_map/psum | solution.py:84
  586.0 2.2 fusion.9
  626.5 26.0 %all-gather.6.cloned.1.call-done = bf16[4,1024,256]{2,1,0:T(8,128)(2,1)} async-done(((bf16[4,128,256]{2,1,0:T(8,128)(2,1)}), bf16[4,1024,256]{2,1,0:T(8,128)(2,1)}) %all-gather.6.cloned.1.call-update) | async-done | bytes 2097168 | tf_op jit(solution)/shard_map/all_gather | solution.py:89
  652.5 5.5 convolution_bitcast_fusion.4
  658.6 35.7 %all-gather.12.cloned.1.call-done = bf16[2,1024,256]{2,1,0:T(8,128)(2,1)} async-done(((bf16[2,128,256]{2,1,0:T(8,128)(2,1)}), bf16[2,1024,256]{2,1,0:T(8,128)(2,1)}) %all-gather.12.cloned.1.call-update) | async-done | bytes 1048592 | tf_op jit(solution)/shard_map/all_gather | solution.py:91
  694.2 13.6 %convolution_bitcast_fusion = f32[2,4000,256]{2,1,0:T(8,128)} fusion(bf16[2,4000,1024]{2,1,0:T(8,128)(2,1)} %param.26, bf16[2,1024,256]{2,1,0:T(8,128)(2,1)} %all-gather.12.cloned.1.call-done), kind=kOutput, calls=%fused_computation.2 | convolution fusion | flops 4194304000 | bytes 25624576 | tf_op jit(solution)/shard_map/smc,scr->smr/dot_general | solution.py:94
  710.1 35.2 %all-gather.10.cloned.1.call-done = bf16[4,1024,256]{2,1,0:T(8,128)(2,1)} async-done(((bf16[4,128,256]{2,1,0:T(8,128)(2,1)}), bf16[4,1024,256]{2,1,0:T(8,128)(2,1)}) %all-gather.10.cloned.1.call-update) | async-done | bytes 2097168 | tf_op jit(solution)/shard_map/all_gather | solution.py:90
  745.3 2.4 convolution_bitcast_fusion.5
  748.8 29.5 %reduce-scatter.8.cloned.1.call-done = f32[4,128,256]{1,2,0:T(8,128)} async-done(((f32[4,512,256]{1,2,0:T(8,128)}), f32[4,128,256]{1,2,0:T(8,128)}) %reduce-scatter.8.cloned.1.call-update) | async-done | bytes 524304 | tf_op jit(solution)/shard_map/reduce_scatter | solution.py:98
  778.4 2.3 divide_convert_fusion.1
  780.7 71.4 %reduce-scatter.14.cloned.1.call-done = f32[2,1000,256]{2,1,0:T(8,128)} async-done(((f32[2,4000,256]{2,1,0:T(8,128)}), f32[2,1000,256]{2,1,0:T(8,128)}) %reduce-scatter.14.cloned.1.call-update) | async-done | bytes 2048016 | tf_op jit(solution)/shard_map/reduce_scatter | solution.py:100
  852.1 6.0 divide_convert_fusion
  859.4 28.7 %all-reduce.9.cloned.1.call-done = f32[4,128,256]{2,0,1:T(4,128)} async-done(((f32[4,128,256]{2,0,1:T(4,128)}), f32[4,128,256]{2,0,1:T(4,128)}) %all-reduce.9.cloned.1.call-update) | async-done | bytes 524304
  890.7 5.9 all_gather.21
  896.7 3.0 subtract_convert_fusion.2
  901.7 5.4 all-gather.8.cloned.1.call-done
  907.2 6.4 subtract_convert_fusion.1
  913.6 29.5 %all-gather.14.cloned.1.call-done = bf16[2,4000,256]{2,1,0:T(8,128)(2,1)} async-done(((bf16[2,1000,256]{2,1,0:T(8,128)(2,1)}), bf16[2,4000,256]{2,1,0:T(8,128)(2,1)}) %all-gather.14.cloned.1.call-update) | async-done | bytes 4096016 | tf_op jit(solution)/shard_map/all_gather | solution.py:108
  943.1 13.3 %subtract_convert_fusion = bf16[2,4000,1024]{2,1,0:T(8,128)(2,1)} fusion(bf16[2,4000,1024]{2,1,0:T(8,128)(2,1)} %param.25, bf16[2,4000,256]{2,1,0:T(8,128)(2,1)} %all-gather.14.cloned.1.call-done, bf16[2,1024,256]{2,1,0:T(8,128)(2,1)S(1)} %copy-done.20), kind=kOutput, calls=%fused_computation | convolution fusion | flops 4235264000 | bytes 37912576 | tf_op jit(solution)/shard_map/smr,scr->smc/dot_general | solution.py:112
  (121 shorter events, 52.5 us)
Async XLA Ops:
  7.2 12.5 %copy-start = (bf16[4,1024,256]{2,1,0:T(8,128)(2,1)S(1)}, bf16[4,1024,256]{2,1,0:T(8,128)(2,1)}, u32[]{:S(2)}) copy-start(bf16[4,1024,256]{2,1,0:T(8,128)(2,1)} %param.19) | copy-start | bytes 6291460
  7.2 127.1 %all-reduce.15.cloned.1.call-start = ((), (), s32[]{:S(2)}) async-start(), calls=%async_computation.18 | async-start | bytes 10813440 | tf_op jit(solution)/shard_map/psum | solution.py:70
  19.7 4.6 copy-start.2
  19.7 4.6 copy-start.12
  25.9 189.7 %reduce-scatter.12.cloned.1.call-start = ((), (), s32[]{:S(2)}) async-start(), calls=%async_computation.11 | async-start | bytes 2359296 | tf_op jit(solution)/shard_map/reduce_scatter | solution.py:82
  147.2 1.2 copy-start.14
  147.2 160.5 %reduce-scatter.6.cloned.1.call-start = ((), (), s32[]{:S(2)}) async-start(), calls=%async_computation.5 | async-start | bytes 4718592 | tf_op jit(solution)/shard_map/reduce_scatter | solution.py:80
  153.9 246.0 %reduce-scatter.10.cloned.1.call-start = ((), (), s32[]{:S(2)}) async-start(), calls=%async_computation.9 | async-start | bytes 4718592 | tf_op jit(solution)/shard_map/reduce_scatter | solution.py:81
  157.6 306.1 %all-reduce.13.cloned.1.call-start = ((), (), s32[]{:S(2)}) async-start(), calls=%async_computation.17 | async-start | bytes 5242880 | tf_op jit(solution)/shard_map/psum | solution.py:84
  403.1 181.6 %all-reduce.11.cloned.1.call-start = ((), (), s32[]{:S(2)}) async-start(), calls=%async_computation.16 | async-start | bytes 5242880 | tf_op jit(solution)/shard_map/psum | solution.py:84
  463.7 188.9 %all-gather.6.cloned.1.call-start = ((), (), s32[]{:S(2)}) async-start(), calls=%async_computation.6 | async-start | bytes 2359296 | tf_op jit(solution)/shard_map/all_gather | solution.py:89
  463.8 140.2 %copy-start.10 = (f32[256,256]{1,0:T(8,128)}, f32[256,256]{1,0:T(8,128)S(1)}, u32[]{:S(2)}) copy-start(f32[256,256]{1,0:T(8,128)S(1)} %fusion.38) | copy-start | bytes 786436
  584.6 3.6 copy-start.4
  584.6 5.2 copy-start.5
  602.1 2.6 copy-start.7
  603.9 90.3 %all-gather.12.cloned.1.call-start = ((), (), s32[]{:S(2)}) async-start(), calls=%async_computation.12 | async-start | bytes 1179648 | tf_op jit(solution)/shard_map/all_gather | solution.py:91
  608.7 1.4 copy-start.11
  616.4 128.9 %all-gather.10.cloned.1.call-start = ((), (), s32[]{:S(2)}) async-start(), calls=%async_computation.10 | async-start | bytes 2359296 | tf_op jit(solution)/shard_map/all_gather | solution.py:90
  626.5 151.9 %reduce-scatter.8.cloned.1.call-start = ((), (), s32[]{:S(2)}) async-start(), calls=%async_computation.7 | async-start | bytes 2621440 | tf_op jit(solution)/shard_map/reduce_scatter | solution.py:98
  658.1 194.0 %reduce-scatter.14.cloned.1.call-start = ((), (), s32[]{:S(2)}) async-start(), calls=%async_computation.13 | async-start | bytes 10240000 | tf_op jit(solution)/shard_map/reduce_scatter | solution.py:100
  707.9 1.2 copy-start.16
  707.9 37.4 %copy-start.3 = (bf16[4,128,1024]{2,1,0:T(8,128)(2,1)S(1)}, bf16[4,128,1024]{2,1,0:T(8,128)(2,1)}, u32[]{:S(2)}) copy-start(bf16[4,128,1024]{2,1,0:T(8,128)(2,1)} %param.21) | copy-start | bytes 3145732
  707.9 180.2 %all-reduce.9.cloned.1.call-start = ((), (), s32[]{:S(2)}) async-start(), calls=%async_computation.15 | async-start | bytes 1048576
  748.8 158.4 %all-gather.8.cloned.1.call-start = ((), (), s32[]{:S(2)}) async-start(), calls=%async_computation.8 | async-start | bytes 1310720 | tf_op jit(solution)/shard_map/all_gather | solution.py:106
  780.6 77.5 %copy-start.21 = (u32[32]{0:T(128)S(1)}, u32[32]{0:T(128)}, u32[]{:S(2)}) copy-start(u32[32]{0:T(128)} %constant.11) | copy-start | bytes 388
  780.7 107.5 %copy-start.18 = (f32[4,32,256]{2,1,0:T(8,128)S(1)}, f32[4,32,256]{2,1,0:T(8,128)}, u32[]{:S(2)}) copy-start(f32[4,32,256]{2,1,0:T(8,128)} %param.22) | copy-start | bytes 393220
  780.7 107.5 %copy-start.19 = (f32[4,32,256]{2,1,0:T(8,128)S(1)}, f32[4,32,256]{2,1,0:T(8,128)}, u32[]{:S(2)}) copy-start(f32[4,32,256]{2,1,0:T(8,128)} %param.23) | copy-start | bytes 393220
  780.7 162.4 %all-gather.14.cloned.1.call-start = ((), (), s32[]{:S(2)}) async-start(), calls=%async_computation.14 | async-start | bytes 5120000 | tf_op jit(solution)/shard_map/all_gather | solution.py:108
  858.1 38.6 %copy-start.6 = (bf16[4,1024,256]{2,1,0:T(8,128)(2,1)S(1)}, bf16[4,1024,256]{2,1,0:T(8,128)(2,1)}, u32[]{:S(2)}) copy-start(bf16[4,1024,256]{2,1,0:T(8,128)(2,1)} %all-gather.10.cloned.1.call-done) | copy-start | bytes 6291460
  899.7 7.4 copy-start.13
  901.7 41.4 %copy-start.20 = (bf16[2,1024,256]{2,1,0:T(8,128)(2,1)S(1)}, bf16[2,1024,256]{2,1,0:T(8,128)(2,1)}, u32[]{:S(2)}) copy-start(bf16[2,1024,256]{2,1,0:T(8,128)(2,1)} %all-gather.12.cloned.1.call-done) | copy-start | bytes 3145732
  943.1 13.3 %copy-start.1 = (bf16[4,1024,256]{2,1,0:T(8,128)(2,1)S(1)}, bf16[4,1024,256]{2,1,0:T(8,128)(2,1)}, u32[]{:S(2)}) copy-start(bf16[4,1024,256]{2,1,0:T(8,128)(2,1)} %param.19) | copy-start | bytes 6291460
  (4 other events, 4.4 us)
Sparse Core Ops, SparseCore 0:
  26.0 108.2 all-reduce.14
  147.3 68.2 reduce-scatter.11
  220.2 87.4 reduce-scatter.5
  311.7 88.0 reduce-scatter.9
  403.5 60.0 all-reduce.12
  467.9 116.6 all-reduce.10
  604.1 48.4 all-gather.5
  655.5 38.6 all-gather.11
  697.2 48.0 all-gather.9
  748.4 29.9 reduce-scatter.7
  781.6 70.5 reduce-scatter.13
  854.9 33.2 all-reduce.8
  890.3 16.8 all-gather.7
  909.1 33.9 all-gather.13
